TPU v7x, 32 devices: a whole 2x2x4 slice. The times are simulated.
32 devices in a mesh: bin: 2 (over y), row: 4 (over x, core), col: 4 (over z).
Axes of the slice: x: 2, y: 2, z: 4, core: 2. Of those that a mesh axis runs over, the one named last changes fastest.
Arguments:
- snapshots: bfloat16 [4096, 16, 64], P('row', 'bin', 'col'), may hold values from -6 to 6
- focus_in: bfloat16 [16, 4096, 128], P('bin', 'row'), may hold values from -0.09375 to 0.09375
- focus_out: bfloat16 [16, 4096, 128], P('bin', 'row'), may hold values from -0.5 to 0.5
- start_basis: float32 [4096, 128], replicated, may hold values from -6 to 6
Outputs:
- covariance: float32 [4096, 4096], P('col', 'row')
- basis_out: float32 [4096, 128], P(('row', 'col'))
All inputs are finite; a program needn't handle non-finite values.
Results may differ from a plain program's by a relative error of at most 0.0045.
Values may be sent and summed in bfloat16 or wider, within the bound.
No kernel may reach another device: no remote copies, remote signals or barrier semaphores. Data moves between devices by JAX's collectives and lax.ppermute only.
A program may use at most 128 MiB of HBM per device.

v0:
```python
import math
import jax
import jax.numpy as jnp
from jax import lax
from jax.sharding import PartitionSpec as P

ITERS = 2


def _transpose_pairs(row_count, col_count):
    return [
        (i * col_count + j, j * row_count + i)
        for i in range(row_count)
        for j in range(col_count)
        if i != j
    ]


def _qr_step(image, gram_axis):
    gram_part = jnp.dot(
        image.T, image, precision=lax.Precision.HIGHEST, preferred_element_type=jnp.float32
    )
    gram_matrix = lax.psum(gram_part, gram_axis)
    lower_factor = jnp.linalg.cholesky(gram_matrix)
    return jax.scipy.linalg.solve_triangular(lower_factor, image.T, lower=True).T


def shards(snapshots, focus_in, focus_out, start_basis):
    rows_here, bins_here, snaps_here = snapshots.shape
    bin_count = lax.axis_size("bin")
    row_count = lax.axis_size("row")
    col_count = lax.axis_size("col")
    col_here = lax.axis_index("col")
    row_here = lax.axis_index("row")
    partial_proj = jnp.einsum(
        "mbs,bmr->brs", snapshots, focus_in, preferred_element_type=jnp.float32
    )
    projected = lax.psum(partial_proj, "row").astype(jnp.bfloat16)
    lifted = jnp.einsum("bmr,brs->mbs", focus_out, projected, preferred_element_type=jnp.float32)
    focused = (snapshots.astype(jnp.float32) + lifted).astype(jnp.bfloat16)
    columns = bins_here * snaps_here
    local_rows = focused.reshape(rows_here, columns)
    array_size = rows_here * row_count
    col_block = array_size // col_count
    scaling = 1.0 / (columns * col_count * bin_count)
    right_rows = lax.all_gather(local_rows, ("bin", "col"), axis=0, tiled=False)
    if row_count == col_count:
        swapped = lax.ppermute(local_rows, ("row", "col"), _transpose_pairs(row_count, col_count))
        swapped = jnp.where(row_here == col_here, local_rows, swapped)
        left_rows = lax.all_gather(swapped, ("bin", "row"), axis=0, tiled=False)
    else:
        every_row = lax.all_gather(right_rows, "row", axis=1, tiled=True)
        left_rows = lax.dynamic_slice_in_dim(every_row, col_here * col_block, col_block, 1)
    covariance = (
        lax.dot_general(
            left_rows, right_rows, (((0, 2), (0, 2)), ((), ())), preferred_element_type=jnp.float32
        )
        * scaling
    )
    basis_rows = lax.dynamic_slice_in_dim(start_basis, row_here * rows_here, rows_here, 0)
    on_rows = True
    for sweep_index in range(ITERS):
        if on_rows:
            partial_image = jnp.dot(
                covariance,
                basis_rows,
                precision=lax.Precision.HIGHEST,
                preferred_element_type=jnp.float32,
            )
            image = lax.psum(partial_image, "row")
            basis_rows = _qr_step(image, "col")
        else:
            partial_image = lax.dot_general(
                covariance,
                basis_rows,
                (((0,), (0,)), ((), ())),
                precision=lax.Precision.HIGHEST,
                preferred_element_type=jnp.float32,
            )
            image = lax.psum(partial_image, "col")
            basis_rows = _qr_step(image, "row")
        on_rows = not on_rows
    if not on_rows:
        swapped = lax.ppermute(basis_rows, ("row", "col"), _transpose_pairs(row_count, col_count))
        basis_rows = jnp.where(row_here == col_here, basis_rows, swapped)
    out_rows = array_size // (row_count * col_count)
    basis_out = lax.dynamic_slice_in_dim(basis_rows, col_here * out_rows, out_rows, 0) * math.sqrt(
        array_size
    )
    return (covariance, basis_out)


def solution(mesh):
    in_specs = (P("row", "bin", "col"), P("bin", "row", None), P("bin", "row", None), P())
    out_specs = (P("col", "row"), P(("row", "col"), None))
    return jax.shard_map(shards, mesh=mesh, in_specs=in_specs, out_specs=out_specs, check_vma=False)
```

profile of v0, /device:TPU:0, one launch (start us, length us, event | category | flops | bytes accessed | tf_op | source)
XLA Modules:
  0.0 343.7 jit_solution(17615606288194781556)
XLA Ops:
  7.2 2.2 fusion.21
  9.4 13.4 %psum.35 = bf16[8,128,16]{1,2,0:T(8,128)(2,1)S(1)} all-reduce(f32[8,128,16]{1,2,0:T(8,128)S(1)} %fusion.21), channel_id=1, replica_groups=mesh['bin'=2,'row'=4,'col'=4] {'row'}, use_global_device_ids=true, to_apply=%region_0.0 | all-reduce | flops 16384 | bytes 98304 | tf_op jit(solution)/shard_map/psum | solution.py:38
  22.9 0.6 fusion.1
  23.6 0.7 collective-permute-start
  24.3 0.8 broadcast_select_fusion
  25.1 0.8 copy.14
  26.0 42.0 %all-gather.6.cloned.1.call-done = bf16[8192,128]{0,1:T(8,128)(2,1)} async-done(((bf16[1024,128]{0,1:T(8,128)(2,1)}), bf16[8192,128]{0,1:T(8,128)(2,1)}) %all-gather.6.cloned.1.call-update) | async-done | bytes 2097168 | tf_op jit(solution)/shard_map/all_gather | solution.py:50
  68.0 4.1 %copy.13 = bf16[8192,128]{1,0:T(8,128)(2,1)} copy(bf16[8192,128]{0,1:T(8,128)(2,1)} %all-gather.6.cloned.1.call-done) | data formatting | bytes 4194304 | tf_op jit(solution)/shard_map/all_gather | solution.py:50
  72.0 47.2 %all-gather.4.cloned.1.call-done = bf16[8,1024,128]{2,1,0:T(8,128)(2,1)} async-done(((bf16[1,1024,128]{2,1,0:T(8,128)(2,1)}), bf16[8,1024,128]{2,1,0:T(8,128)(2,1)}) %all-gather.4.cloned.1.call-update) | async-done | bytes 2097168 | tf_op jit(solution)/shard_map/all_gather | solution.py:46
  119.2 4.6 %bitcast_multiply_fusion = f32[1024,1024]{1,0:T(8,128)S(1)} fusion(bf16[8,1024,128]{2,1,0:T(8,128)(2,1)} %bitcast.53, bf16[8,1024,128]{2,1,0:T(8,128)(2,1)} %all-gather.4.cloned.1.call-done), kind=kOutput, calls=%fused_computation | convolution fusion | flops 2148532224 | bytes 8388608 | tf_op jit(solution)/shard_map/dot_general | solution.py:55
  123.8 2.0 copy-done.1
  125.8 5.3 %fusion.6 = f32[1024,128]{1,0:T(8,128)} fusion(f32[1024,1024]{1,0:T(8,128)S(1)} %bitcast_multiply_fusion, f32[4096,128]{1,0:T(8,128)} %param.10, s32[]{:T(128)S(6)} %select_n.19), kind=kOutput, calls=%fused_computation.8 | convolution fusion | flops 1610612736 | bytes 5242884 | tf_op jit(solution)/shard_map/dot_general | solution.py:64
  131.2 32.0 %all-reduce.5.cloned.1.call-done = f32[1024,128]{1,0:T(8,128)} async-done(((f32[1024,128]{1,0:T(8,128)}), f32[1024,128]{1,0:T(8,128)}) %all-reduce.5.cloned.1.call-update) | async-done | bytes 524304 | tf_op jit(solution)/shard_map/psum | solution.py:70
  163.2 2.8 fusion.18
  166.3 34.3 %all-reduce.7.cloned.1.call-done = f32[128,128]{0,1:T(8,128)} async-done(((f32[128,128]{0,1:T(8,128)}), f32[128,128]{0,1:T(8,128)}) %all-reduce.7.cloned.1.call-update) | async-done | bytes 65552 | tf_op jit(solution)/shard_map/psum | solution.py:23
  200.6 0.9 copy.16
  201.5 0.9 fusion.13
  202.4 11.7 %cholesky.44 = f32[128,128]{1,0:T(8,128)S(1)} custom-call(f32[128,128]{1,0:T(8,128)S(1)} %fusion.13), custom_call_target="Cholesky" | custom-call | tf_op jit(solution)/shard_map/jit(cholesky)/cholesky | solution.py:24
  214.8 0.7 fusion.8
  215.5 9.8 %custom-call.6 = f32[1,128,128]{1,2,0:T(8,128)S(1)} custom-call(f32[1,128,128]{2,1,0:T(8,128)S(1)} %fusion.8), custom_call_target="InvertDiagBlocksLowerTriangular" | custom-call | tf_op jit(solution)/shard_map/jit(_solve_triangular)/triangular_solve | solution.py:25
  225.3 1.7 fusion.4
  227.0 9.9 %fusion.19 = f32[1024,128]{1,0:T(8,128)} fusion(f32[1024,1024]{1,0:T(8,128)} %copy-done.1, f32[128,1024]{1,0:T(8,128)S(1)} %fusion.4), kind=kOutput, calls=%fused_computation.32 | convolution fusion | flops 1610612736 | bytes 5242880 | tf_op jit(solution)/shard_map/dot_general | solution.py:73
  236.9 38.5 %all-reduce.9.cloned.1.call-done = f32[1024,128]{1,0:T(8,128)} async-done(((f32[1024,128]{1,0:T(8,128)}), f32[1024,128]{1,0:T(8,128)}) %all-reduce.9.cloned.1.call-update) | async-done | bytes 524304 | tf_op jit(solution)/shard_map/psum | solution.py:80
  275.4 2.8 fusion.20
  278.2 31.5 %all-reduce.11.cloned.1.call-done = f32[128,128]{0,1:T(8,128)} async-done(((f32[128,128]{0,1:T(8,128)}), f32[128,128]{0,1:T(8,128)}) %all-reduce.11.cloned.1.call-update) | async-done | bytes 65552 | tf_op jit(solution)/shard_map/psum | solution.py:23
  309.7 0.9 copy.18
  310.7 0.9 fusion.11
  311.5 11.7 %cholesky.55 = f32[128,128]{1,0:T(8,128)S(1)} custom-call(f32[128,128]{1,0:T(8,128)S(1)} %fusion.11), custom_call_target="Cholesky" | custom-call | tf_op jit(solution)/shard_map/jit(cholesky)/cholesky | solution.py:24
  323.9 0.7 fusion.9
  324.6 9.8 %custom-call.7 = f32[1,128,128]{1,2,0:T(8,128)S(1)} custom-call(f32[1,128,128]{2,1,0:T(8,128)S(1)} %fusion.9), custom_call_target="InvertDiagBlocksLowerTriangular" | custom-call | tf_op jit(solution)/shard_map/jit(_solve_triangular)/triangular_solve | solution.py:25
  334.4 1.7 fusion.2
  336.1 0.8 copy.19
  (23 shorter events, 1.9 us)
Async XLA Ops:
  7.2 15.7 %copy-start = (bf16[8,1024,128]{2,1,0:T(8,128)(2,1)S(1)}, bf16[8,1024,128]{2,1,0:T(8,128)(2,1)}, u32[]{:S(2)}) copy-start(bf16[8,1024,128]{2,1,0:T(8,128)(2,1)} %param.9) | copy-start | bytes 6291460
  7.2 15.7 %copy-start.2 = (bf16[1024,8,16]{0,2,1:T(8,128)(2,1)S(1)}, bf16[1024,8,16]{0,2,1:T(8,128)(2,1)}, u32[]{:S(2)}) copy-start(bf16[1024,8,16]{0,2,1:T(8,128)(2,1)} %param.7) | copy-start | bytes 786436
  7.2 60.8 %all-gather.6.cloned.1.call-start = ((), (), s32[]{:S(2)}) async-start(), calls=%async_computation.5 | async-start | bytes 2359296 | tf_op jit(solution)/shard_map/all_gather | solution.py:50
  23.6 0.7 collective-permute-start
  25.0 94.2 %all-gather.4.cloned.1.call-start = ((), (), s32[]{:S(2)}) async-start(), calls=%async_computation | async-start | bytes 2359296 | tf_op jit(solution)/shard_map/all_gather | solution.py:46
  25.9 137.3 %all-reduce.5.cloned.1.call-start = ((), (), s32[]{:S(2)}) async-start(), calls=%async_computation.1 | async-start | bytes 1048576 | tf_op jit(solution)/shard_map/psum | solution.py:70
  123.8 2.0 copy-start.1
  131.1 69.5 %all-reduce.7.cloned.1.call-start = ((), (), s32[]{:S(2)}) async-start(), calls=%async_computation.2 | async-start | bytes 131072 | tf_op jit(solution)/shard_map/psum | solution.py:23
  166.0 109.3 %all-reduce.9.cloned.1.call-start = ((), (), s32[]{:S(2)}) async-start(), calls=%async_computation.3 | async-start | bytes 1048576 | tf_op jit(solution)/shard_map/psum | solution.py:80
  236.9 72.9 %all-reduce.11.cloned.1.call-start = ((), (), s32[]{:S(2)}) async-start(), calls=%async_computation.4 | async-start | bytes 131072 | tf_op jit(solution)/shard_map/psum | solution.py:23
Sparse Core Ops, SparseCore 0:
  25.2 42.7 all-gather.5
  70.1 49.0 all-gather.3
  131.2 31.9 all-reduce.4
  166.2 34.3 all-reduce.6
  237.0 38.3 all-reduce.8
  278.4 31.3 all-reduce.10
where the time goes:
time: 344 us
  waiting for transfers between devices  226 us (66%)
  other arithmetic  48.2 us (14%)
  matrix products  31.6 us (9%)
  between operations  14.3 us (4%)
  blocking collectives  13.4 us (4%)
  local copies, waits for them, and re-layouts  9.52 us (3%)
    psum x2, waiting for transfers between devices, _qr_step(): gram_matrix = lax.psum(gram_part, gram_axis)  65.8 us
    all_gather x1, waiting for transfers between devices, shards(): right_rows = lax.all_gather(local_rows, ('bin', 'col'), axis=0, tiled=False)  47.2 us
    all_gather x1, waiting for transfers between devices, shards(): left_rows = lax.all_gather(swapped, ('bin', 'row'), axis=0, tiled=False)  42 us
    psum x1, waiting for transfers between devices, shards(): image = lax.psum(partial_image, 'col')  38.5 us
    psum x1, waiting for transfers between devices, shards(): image = lax.psum(partial_image, 'row')  32 us
    another operation x6, other arithmetic, _qr_step(): lower_factor = jnp.linalg.cholesky(gram_matrix)  24.8 us
    another operation x4, other arithmetic, _qr_step(): jax.scipy.linalg.solve_triangular(lower_factor, image.T, lower=True)  20.9 us
    psum x1, blocking collectives, shards(): projected = lax.psum(partial_proj, 'row').astype(jnp.bfloat16)  13.4 us
  transfers between devices with their start and end apart: 7, of which 6 were waited for; matrix products, arithmetic and copies ran while one was open for 1% of the time, Pallas kernels for 0%

commit v1 on v0

--- a/solution.py
+++ b/solution.py
@@ -67,7 +67,13 @@
                 precision=lax.Precision.HIGHEST,
                 preferred_element_type=jnp.float32,
             )
-            image = lax.psum(partial_image, "row")
+            n_dev = lax.axis_size("row")
+            image, stride = (partial_image, 1)
+            while stride < n_dev:
+                image = image + lax.ppermute(
+                    image, "row", [(i_2, i_2 ^ stride) for i_2 in range(n_dev)]
+                )
+                stride = 2 * stride
             basis_rows = _qr_step(image, "col")
         else:
             partial_image = lax.dot_general(

time: 344 us -> 322 us (0.936)
  waiting for transfers between devices: 226 us -> 206 us
    psum x1 -> x0, waiting for transfers between devices: 32 us -> none  [shards(): image = lax.psum(partial_image, 'row')]
    ppermute x0 -> x2, waiting for transfers between devices: none -> 14.4 us  [shards(): lax.ppermute(image, 'row', [(i_2, i_2 ^ stride) for i_2 in range(n_dev)])]
  transfers between devices with their start and end apart: 7 -> 8, of which waited for: 6 -> 7; matrix products, arithmetic and copies ran while one was open for 1% -> 2% of each run, Pallas kernels for 0% -> 0%
where the time goes in v1:
time: 322 us; the launch traced here: 321 us
  waiting for transfers between devices  206 us (64%)
  other arithmetic  48.2 us (15%)
  matrix products  29 us (9%)
  between operations  14 us (4%)
  blocking collectives  13.4 us (4%)
  local copies, waits for them, and re-layouts  7.51 us (2%)
    psum x2, waiting for transfers between devices, _qr_step(): gram_matrix = lax.psum(gram_part, gram_axis)  64.3 us
    all_gather x1, waiting for transfers between devices, shards(): right_rows = lax.all_gather(local_rows, ('bin', 'col'), axis=0, tiled=False)  47.2 us
    all_gather x1, waiting for transfers between devices, shards(): left_rows = lax.all_gather(swapped, ('bin', 'row'), axis=0, tiled=False)  42 us
    psum x1, waiting for transfers between devices, shards(): image = lax.psum(partial_image, 'col')  38.4 us
    another operation x6, other arithmetic, _qr_step(): lower_factor = jnp.linalg.cholesky(gram_matrix)  24.8 us
    another operation x4, other arithmetic, _qr_step(): jax.scipy.linalg.solve_triangular(lower_factor, image.T, lower=True)  20.9 us
    ppermute x2, waiting for transfers between devices, shards(): lax.ppermute(image, 'row', [(i_2, i_2 ^ stride) for i_2 in range(n_dev)])  14.4 us
    psum x1, blocking collectives, shards(): projected = lax.psum(partial_proj, 'row').astype(jnp.bfloat16)  13.4 us
  transfers between devices with their start and end apart: 8, of which 7 were waited for; matrix products, arithmetic and copies ran while one was open for 2% of the time, Pallas kernels for 0%

profile of v1, /device:TPU:0, one launch (start us, length us, event | category | flops | bytes accessed | tf_op | source)
XLA Modules:
  0.0 321.2 jit_solution(5326700686500446899)
XLA Ops:
  7.2 2.2 fusion.23
  9.4 13.4 %psum.28 = bf16[8,128,16]{1,2,0:T(8,128)(2,1)S(1)} all-reduce(f32[8,128,16]{1,2,0:T(8,128)S(1)} %fusion.23), channel_id=1, replica_groups=mesh['bin'=2,'row'=4,'col'=4] {'row'}, use_global_device_ids=true, to_apply=%region_0.0 | all-reduce | flops 16384 | bytes 98304 | tf_op jit(solution)/shard_map/psum | solution.py:38
  22.9 0.6 fusion.1
  23.6 0.7 collective-permute-start
  24.3 0.8 broadcast_select_fusion
  25.1 0.8 copy.14
  26.0 42.0 %all-gather.6.cloned.1.call-done = bf16[8192,128]{0,1:T(8,128)(2,1)} async-done(((bf16[1024,128]{0,1:T(8,128)(2,1)}), bf16[8192,128]{0,1:T(8,128)(2,1)}) %all-gather.6.cloned.1.call-update) | async-done | bytes 2097168 | tf_op jit(solution)/shard_map/all_gather | solution.py:50
  68.0 4.1 %copy.13 = bf16[8192,128]{1,0:T(8,128)(2,1)} copy(bf16[8192,128]{0,1:T(8,128)(2,1)} %all-gather.6.cloned.1.call-done) | data formatting | bytes 4194304 | tf_op jit(solution)/shard_map/all_gather | solution.py:50
  72.0 47.2 %all-gather.4.cloned.1.call-done = bf16[8,1024,128]{2,1,0:T(8,128)(2,1)} async-done(((bf16[1,1024,128]{2,1,0:T(8,128)(2,1)}), bf16[8,1024,128]{2,1,0:T(8,128)(2,1)}) %all-gather.4.cloned.1.call-update) | async-done | bytes 2097168 | tf_op jit(solution)/shard_map/all_gather | solution.py:46
  119.2 4.6 %bitcast_multiply_fusion = f32[1024,1024]{1,0:T(8,128)S(1)} fusion(bf16[8,1024,128]{2,1,0:T(8,128)(2,1)} %bitcast.51, bf16[8,1024,128]{2,1,0:T(8,128)(2,1)} %all-gather.4.cloned.1.call-done), kind=kOutput, calls=%fused_computation | convolution fusion | flops 2148532224 | bytes 8388608 | tf_op jit(solution)/shard_map/dot_general | solution.py:55
  123.8 4.9 %fusion.6 = f32[1024,128]{1,0:T(8,128)S(1)} fusion(f32[1024,1024]{1,0:T(8,128)S(1)} %bitcast_multiply_fusion, f32[4096,128]{1,0:T(8,128)} %param.10, s32[]{:T(128)S(6)} %select_n.19), kind=kOutput, calls=%fused_computation.8 | convolution fusion | flops 1610612736 | bytes 5242884 | tf_op jit(solution)/shard_map/dot_general | solution.py:64
  128.8 1.9 collective-permute-done.1
  130.7 1.5 collective-permute-start.2
  132.3 12.5 %collective-permute-done.2 = f32[1024,128]{1,0:T(8,128)S(1)} collective-permute-done((f32[1024,128]{1,0:T(8,128)S(1)}, f32[1024,128]{1,0:T(8,128)S(1)}, u32[]{:S(2)}, u32[]{:S(2)}) %collective-permute-start.2) | collective-permute-done | bytes 524320 | tf_op jit(solution)/shard_map/ppermute | solution.py:73
  144.8 1.6 fusion.9
  146.7 32.8 %all-reduce.4.cloned.1.call-done = f32[128,128]{0,1:T(8,128)} async-done(((f32[128,128]{0,1:T(8,128)}), f32[128,128]{0,1:T(8,128)}) %all-reduce.4.cloned.1.call-update) | async-done | bytes 65552 | tf_op jit(solution)/shard_map/psum | solution.py:23
  179.4 0.9 copy.16
  180.4 0.9 fusion.16
  181.2 11.7 %cholesky.44 = f32[128,128]{1,0:T(8,128)S(1)} custom-call(f32[128,128]{1,0:T(8,128)S(1)} %fusion.16), custom_call_target="Cholesky" | custom-call | tf_op jit(solution)/shard_map/jit(cholesky)/cholesky | solution.py:24
  193.6 0.7 fusion.11
  194.3 9.8 %custom-call.6 = f32[1,128,128]{1,2,0:T(8,128)S(1)} custom-call(f32[1,128,128]{2,1,0:T(8,128)S(1)} %fusion.11), custom_call_target="InvertDiagBlocksLowerTriangular" | custom-call | tf_op jit(solution)/shard_map/jit(_solve_triangular)/triangular_solve | solution.py:25
  204.7 9.9 %fusion.21 = f32[1024,128]{1,0:T(8,128)} fusion(f32[1024,1024]{1,0:T(8,128)} %copy-done.1, f32[128,1024]{1,0:T(8,128)S(1)} %fusion.4), kind=kOutput, calls=%fused_computation.34 | convolution fusion | flops 1610612736 | bytes 5242880 | tf_op jit(solution)/shard_map/dot_general | solution.py:79
  214.7 38.4 %all-reduce.6.cloned.1.call-done = f32[1024,128]{1,0:T(8,128)} async-done(((f32[1024,128]{1,0:T(8,128)}), f32[1024,128]{1,0:T(8,128)}) %all-reduce.6.cloned.1.call-update) | async-done | bytes 524304 | tf_op jit(solution)/shard_map/psum | solution.py:86
  253.1 2.8 fusion.22
  256.0 31.5 %all-reduce.8.cloned.1.call-done = f32[128,128]{0,1:T(8,128)} async-done(((f32[128,128]{0,1:T(8,128)}), f32[128,128]{0,1:T(8,128)}) %all-reduce.8.cloned.1.call-update) | async-done | bytes 65552 | tf_op jit(solution)/shard_map/psum | solution.py:23
  287.5 0.9 copy.18
  288.4 0.9 fusion.14
  289.3 11.7 %cholesky.55 = f32[128,128]{1,0:T(8,128)S(1)} custom-call(f32[128,128]{1,0:T(8,128)S(1)} %fusion.14), custom_call_target="Cholesky" | custom-call | tf_op jit(solution)/shard_map/jit(cholesky)/cholesky | solution.py:24
  301.7 0.7 fusion.12
  302.3 9.8 %custom-call.7 = f32[1,128,128]{1,2,0:T(8,128)S(1)} custom-call(f32[1,128,128]{2,1,0:T(8,128)S(1)} %fusion.12), custom_call_target="InvertDiagBlocksLowerTriangular" | custom-call | tf_op jit(solution)/shard_map/jit(_solve_triangular)/triangular_solve | solution.py:25
  312.2 1.7 fusion.2
  313.9 0.8 copy.19
  (25 shorter events, 2.6 us)
Async XLA Ops:
  7.2 15.7 %copy-start = (bf16[8,1024,128]{2,1,0:T(8,128)(2,1)S(1)}, bf16[8,1024,128]{2,1,0:T(8,128)(2,1)}, u32[]{:S(2)}) copy-start(bf16[8,1024,128]{2,1,0:T(8,128)(2,1)} %param.9) | copy-start | bytes 6291460
  7.2 15.7 %copy-start.2 = (bf16[1024,8,16]{0,2,1:T(8,128)(2,1)S(1)}, bf16[1024,8,16]{0,2,1:T(8,128)(2,1)}, u32[]{:S(2)}) copy-start(bf16[1024,8,16]{0,2,1:T(8,128)(2,1)} %param.7) | copy-start | bytes 786436
  7.2 60.8 %all-gather.6.cloned.1.call-start = ((), (), s32[]{:S(2)}) async-start(), calls=%async_computation.4 | async-start | bytes 2359296 | tf_op jit(solution)/shard_map/all_gather | solution.py:50
  23.6 0.7 collective-permute-start
  25.0 94.2 %all-gather.4.cloned.1.call-start = ((), (), s32[]{:S(2)}) async-start(), calls=%async_computation | async-start | bytes 2359296 | tf_op jit(solution)/shard_map/all_gather | solution.py:46
  25.9 153.5 %all-reduce.4.cloned.1.call-start = ((), (), s32[]{:S(2)}) async-start(), calls=%async_computation.1 | async-start | bytes 131072 | tf_op jit(solution)/shard_map/psum | solution.py:23
  123.8 4.9 %copy-start.1 = (f32[1024,1024]{1,0:T(8,128)}, f32[1024,1024]{1,0:T(8,128)S(1)}, u32[]{:S(2)}) copy-start(f32[1024,1024]{1,0:T(8,128)S(1)} %bitcast_multiply_fusion) | copy-start | bytes 12582916
  128.7 2.0 collective-permute-start.1
  130.7 14.0 %collective-permute-start.2 = (f32[1024,128]{1,0:T(8,128)S(1)}, f32[1024,128]{1,0:T(8,128)S(1)}, u32[]{:S(2)}, u32[]{:S(2)}) collective-permute-start(f32[1024,128]{1,0:T(8,128)S(1)} %add.34), channel_id=1, source_target_pairs={{0,8},{4,12},{8,0},{12,4},{1,9},{5,13},{9,1},{13,5},{2,10},{6,14},... | collective-permute-start | bytes 1572872 | tf_op jit(solution)/shard_map/ppermute | solution.py:73
  146.4 106.7 %all-reduce.6.cloned.1.call-start = ((), (), s32[]{:S(2)}) async-start(), calls=%async_computation.2 | async-start | bytes 1048576 | tf_op jit(solution)/shard_map/psum | solution.py:86
  214.6 72.9 %all-reduce.8.cloned.1.call-start = ((), (), s32[]{:S(2)}) async-start(), calls=%async_computation.3 | async-start | bytes 131072 | tf_op jit(solution)/shard_map/psum | solution.py:23
Sparse Core Ops, SparseCore 0:
  25.2 42.7 all-gather.5
  70.1 49.0 all-gather.3
  146.6 32.8 all-reduce.3
  214.8 38.3 all-reduce.5
  256.1 31.3 all-reduce.7
